TPU v7x, 256 devices: a whole 4x4x8 slice. The times are simulated.
256 devices in a mesh: gx: 16 (over z_lo, x, core), gy: 16 (over z_hi, y).
Axes of the slice: x: 4, y: 4, z: 8 (z_hi: 4, z_lo: 2; z = z_hi * 2 + z_lo), core: 2. Of those that a mesh axis runs over, the one named last changes fastest.
Arguments:
- species_field: float32 [4, 1024, 256, 256], P(None, 'gx', 'gy'), may hold values from -400 to 400
- initial: float32 [1024, 128], replicated, may hold values from -6 to 6
Outputs:
- factor: float32 [1024, 128], replicated
- gram_two: float32 [256, 256], replicated
All inputs are finite; a program needn't handle non-finite values.
Results may differ from a plain program's by a relative error of at most 0.0002.
Values sent between devices are 32-bit elements; how exact they have to be, the bound alone decides.
No kernel may reach another device: no remote copies, remote signals or barrier semaphores. Data moves between devices by JAX's collectives and lax.ppermute only.
A program may use at most 128 MiB of HBM per device.

v0:
```python
import math
import jax
import jax.numpy as jnp
from jax import lax
from jax.sharding import PartitionSpec as P

S = 4
NY = 256
NZ = 256
R = 128
SWEEPS = 3


def body(species_field, initial):
    highest = lax.Precision.HIGHEST
    regrouped = lax.all_to_all(species_field, "gx", split_axis=3, concat_axis=1, tiled=True)
    species, rows_x, cols_y, slab_z = regrouped.shape
    fibers = regrouped.reshape(species, rows_x, cols_y * slab_z)
    scale_one = 1.0 / (S * NY * NZ)
    basis = initial
    gram_one = lax.psum(
        jnp.einsum("sxc,swc->xw", fibers, fibers, precision=highest) * scale_one, ("gx", "gy")
    )
    for sweep_index in range(SWEEPS):
        wide = jnp.dot(gram_one, basis, precision=highest, preferred_element_type=jnp.float32)
        square = jnp.dot(wide.T, wide, precision=highest, preferred_element_type=jnp.float32)
        factor_low = jnp.linalg.cholesky(square)
        basis = jax.scipy.linalg.solve_triangular(factor_low, wide.T, lower=True).T
    core_tensor = jnp.einsum("xr,sxc->src", basis, fibers, precision=highest)
    core_blocks = core_tensor.reshape(species, R, cols_y, slab_z)
    blocks = lax.all_to_all(core_blocks, "gy", split_axis=1, concat_axis=2, tiled=True)
    second_part = jnp.einsum("sryz,srwz->yw", blocks, blocks, precision=highest) / (S * R * NZ)
    gram_two = lax.psum(second_part, ("gx", "gy"))
    return (basis * math.sqrt(rows_x), gram_two)


def solution(mesh):
    placed = (P(None, "gx", "gy", None), P())
    return jax.shard_map(body, mesh=mesh, in_specs=placed, out_specs=(P(), P()), check_vma=False)
```

profile of v0, /device:TPU:2, one launch (start us, length us, event | category | flops | bytes accessed | tf_op | source)
XLA Modules:
  0.0 817.2 jit_solution(10671262008300448773)
XLA Ops:
  7.2 9.2 %copy.33 = f32[4,64,16,256]{1,2,0,3:T(8,128)} copy(f32[4,64,16,256]{3,2,1,0:T(8,128)} %param.5) | data formatting | bytes 8388608 | tf_op args[0]
  16.4 13.3 %reshape.24 = f32[16,1,65536]{2,1,0:T(1,128)} reshape(f32[256,4,16,64]{3,2,1,0:T(8,128)} %bitcast.87) | data formatting | bytes 8388608
  29.7 53.2 %all_to_all.33 = f32[16,1,65536]{2,1,0:T(1,128)} all-to-all(f32[16,1,65536]{2,1,0:T(1,128)} %reshape.24), channel_id=1, replica_groups=mesh['gx'=16,'gy'=16] {'gx'}, dimensions={0} | all-to-all | bytes 8388608 | tf_op jit(solution)/shard_map/all_to_all | solution.py:16
  83.4 13.7 %reduce.4 = f32[16,65536]{1,0:T(8,128)} reduce(f32[16,1,65536]{2,1,0:T(1,128)} %all_to_all.33, f32[]{:T(128)} %broadcast.39), dimensions={1}, to_apply=%all_to_all.24.reduce_sub_computation | reduce | bytes 8388612 | tf_op jit(solution)/shard_map/all_to_all | solution.py:16
  97.2 6.9 reshape.25
  104.1 11.4 %copy.35 = f32[4,16,64,16,16]{2,1,4,3,0:T(8,128)} copy(f32[4,16,64,16,16]{2,3,0,4,1:T(8,128)} %bitcast.88) | data formatting | bytes 8388608 | tf_op jit(solution)/shard_map/all_to_all | solution.py:16
  115.5 7.6 reshape.19
  123.1 17.8 %bitcast_multiply_fusion = f32[1024,1024]{1,0:T(8,128)} fusion(f32[4,1024,256]{1,2,0:T(8,128)} %reshape.19), kind=kOutput, calls=%fused_computation | convolution fusion | flops 12885950464 | bytes 8388608 | tf_op jit(solution)/shard_map/sxc,swc->xw/dot_general | solution.py:22
  141.0 273.0 %all-reduce.3.cloned.1.call-done = f32[1024,1024]{1,0:T(8,128)} async-done(((f32[1024,1024]{1,0:T(8,128)}), f32[1024,1024]{1,0:T(8,128)}) %all-reduce.3.cloned.1.call-update) | async-done | bytes 4194320 | tf_op jit(solution)/shard_map/psum | solution.py:21
  414.0 5.6 fusion.21
  420.7 11.7 %cholesky.59 = f32[128,128]{1,0:T(8,128)S(1)} custom-call(f32[128,128]{1,0:T(8,128)S(1)} %fusion.16), custom_call_target="Cholesky" | custom-call | tf_op jit(solution)/shard_map/jit(cholesky)/cholesky | solution.py:27
  433.8 9.8 %custom-call.7 = f32[1,128,128]{1,2,0:T(8,128)S(1)} custom-call(f32[1,128,128]{2,1,0:T(8,128)S(1)} %fusion.8), custom_call_target="InvertDiagBlocksLowerTriangular" | custom-call | tf_op jit(solution)/shard_map/jit(_solve_triangular)/triangular_solve | solution.py:28
  444.2 5.4 fusion.23
  450.8 11.7 %cholesky.70 = f32[128,128]{1,0:T(8,128)S(1)} custom-call(f32[128,128]{1,0:T(8,128)S(1)} %fusion.14), custom_call_target="Cholesky" | custom-call | tf_op jit(solution)/shard_map/jit(cholesky)/cholesky | solution.py:27
  463.8 9.8 %custom-call.8 = f32[1,128,128]{1,2,0:T(8,128)S(1)} custom-call(f32[1,128,128]{2,1,0:T(8,128)S(1)} %fusion.9), custom_call_target="InvertDiagBlocksLowerTriangular" | custom-call | tf_op jit(solution)/shard_map/jit(_solve_triangular)/triangular_solve | solution.py:28
  474.3 5.4 fusion.25
  480.9 11.7 %cholesky.81 = f32[128,128]{1,0:T(8,128)S(1)} custom-call(f32[128,128]{1,0:T(8,128)S(1)} %fusion.12), custom_call_target="Cholesky" | custom-call | tf_op jit(solution)/shard_map/jit(cholesky)/cholesky | solution.py:27
  493.9 9.8 %custom-call.9 = f32[1,128,128]{1,2,0:T(8,128)S(1)} custom-call(f32[1,128,128]{2,1,0:T(8,128)S(1)} %fusion.10), custom_call_target="InvertDiagBlocksLowerTriangular" | custom-call | tf_op jit(solution)/shard_map/jit(_solve_triangular)/triangular_solve | solution.py:28
  504.4 6.5 convolution_bitcast_fusion
  511.1 4.6 copy.43
  515.8 3.5 reshape.26
  519.3 20.9 %all_to_all.34 = f32[16,1,8192]{2,1,0:T(1,128)S(1)} all-to-all(f32[16,1,8192]{2,1,0:T(1,128)S(1)} %reshape.26), channel_id=1, replica_groups=mesh['gx'=16,'gy'=16] {'gy'}, dimensions={0} | all-to-all | bytes 1048576 | tf_op jit(solution)/shard_map/all_to_all | solution.py:31
  544.9 5.6 copy.45
  556.7 251.5 %all-reduce.5.cloned.1.call-done = f32[256,256]{1,0:T(8,128)} async-done(((f32[256,256]{1,0:T(8,128)}), f32[256,256]{1,0:T(8,128)}) %all-reduce.5.cloned.1.call-update) | async-done | bytes 262160 | tf_op jit(solution)/shard_map/psum | solution.py:33
  (36 shorter events, 22.6 us)
Async XLA Ops:
  7.2 406.8 %copy-start = (f32[1024,128]{1,0:T(8,128)S(1)}, f32[1024,128]{1,0:T(8,128)}, u32[]{:S(2)}) copy-start(f32[1024,128]{1,0:T(8,128)} %param.6) | copy-start | bytes 1572868
  7.2 406.8 %all-reduce.3.cloned.1.call-start = ((), (), s32[]{:S(2)}) async-start(), calls=%async_computation.2 | async-start | bytes 8388608 | tf_op jit(solution)/shard_map/psum | solution.py:21
  140.9 667.4 %all-reduce.5.cloned.1.call-start = ((), (), s32[]{:S(2)}) async-start(), calls=%async_computation.3 | async-start | bytes 524288 | tf_op jit(solution)/shard_map/psum | solution.py:33
Sparse Core Ops, SparseCore 0:
  141.0 272.9 all-reduce.2
  555.8 252.4 all-reduce.4
where the time goes:
time: 826 us; the launch traced here: 817 us
  waiting for transfers between devices  525 us (64%)
  other arithmetic  84.2 us (10%)
  blocking collectives  74.2 us (9%)
  local copies, waits for them, and re-layouts  72 us (9%)
  matrix products  47.4 us (6%)
  between operations  14.7 us (2%)
    psum x1, waiting for transfers between devices, body(): lax.psum(jnp.einsum('sxc,swc->xw', fibers, fibers, precision=highest) * s...  273 us
    psum x1, waiting for transfers between devices, body(): gram_two = lax.psum(second_part, ('gx', 'gy'))  252 us
    all_to_all x1, blocking collectives, body(): lax.all_to_all(species_field, 'gx', split_axis=3, concat_axis=1, tiled=True)  53.2 us
    unnamed x9, local copies, waits for them, and re-layouts  38.3 us
    another operation x9, other arithmetic, body(): factor_low = jnp.linalg.cholesky(square)  37.2 us
    another operation x6, other arithmetic, body(): basis = jax.scipy.linalg.solve_triangular(factor_low, wide.T, lower=True).T  31.4 us
    all_to_all x1, blocking collectives, body(): lax.all_to_all(core_blocks, 'gy', split_axis=1, concat_axis=2, tiled=True)  20.9 us
    dot_general x1, matrix products, body(): jnp.einsum('sxc,swc->xw', fibers, fibers, precision=highest) * scale_one  17.8 us
  transfers between devices with their start and end apart: 2, of which 2 were waited for; matrix products, arithmetic and copies ran while one was open for 0% of the time, Pallas kernels for 0%

commit v1 on v0

--- a/solution.py
+++ b/solution.py
@@ -13,7 +13,12 @@
 
 def body(species_field, initial):
     highest = lax.Precision.HIGHEST
-    regrouped = lax.all_to_all(species_field, "gx", split_axis=3, concat_axis=1, tiled=True)
+    regrouped = jnp.concatenate(
+        lax.all_to_all(
+            jnp.stack(jnp.split(species_field, lax.axis_size("gx"), axis=3)), "gx", 0, 0
+        ),
+        axis=1,
+    )
     species, rows_x, cols_y, slab_z = regrouped.shape
     fibers = regrouped.reshape(species, rows_x, cols_y * slab_z)
     scale_one = 1.0 / (S * NY * NZ)

time: 826 us -> 916 us (1.11)
  local copies, waits for them, and re-layouts: 72 us -> 168 us
    unnamed x9 -> x61, local copies, waits for them, and re-layouts: 38.3 us -> 106 us
    split x0 -> x1, local copies, waits for them, and re-layouts: none -> 26.9 us  [body(): jnp.split(species_field, lax.axis_size('gx'), axis=3)]
    all_to_all x2 -> x1, local copies, waits for them, and re-layouts: 12 us -> 0.51 us  [body(): lax.all_to_all(jnp.stack(jnp.split(species_field, lax.axis_size('gx'), ax...]
where the time goes in v1:
time: 916 us; the launch traced here: 912 us
  waiting for transfers between devices  525 us (57%)
  local copies, waits for them, and re-layouts  168 us (18%)
  other arithmetic  84.2 us (9%)
  blocking collectives  74.4 us (8%)
  matrix products  45.9 us (5%)
  between operations  14.6 us (2%)
    psum x1, waiting for transfers between devices, body(): lax.psum(jnp.einsum('sxc,swc->xw', fibers, fibers, precision=highest) * s...  273 us
    psum x1, waiting for transfers between devices, body(): gram_two = lax.psum(second_part, ('gx', 'gy'))  252 us
    unnamed x61, local copies, waits for them, and re-layouts  106 us
    all_to_all x1, blocking collectives, body(): lax.all_to_all(jnp.stack(jnp.split(species_field, lax.axis_size('gx'), ax...  53.2 us
    another operation x9, other arithmetic, body(): factor_low = jnp.linalg.cholesky(square)  37.2 us
    another operation x6, other arithmetic, body(): basis = jax.scipy.linalg.solve_triangular(factor_low, wide.T, lower=True).T  31.4 us
    split x1, local copies, waits for them, and re-layouts, body(): jnp.split(species_field, lax.axis_size('gx'), axis=3)  26.9 us
    all_to_all x1, blocking collectives, body(): lax.all_to_all(core_blocks, 'gy', split_axis=1, concat_axis=2, tiled=True)  21.2 us
  transfers between devices with their start and end apart: 2, of which 2 were waited for; matrix products, arithmetic and copies ran while one was open for 0% of the time, Pallas kernels for 0%

profile of v1, /device:TPU:2, one launch (start us, length us, event | category | flops | bytes accessed | tf_op | source)
XLA Modules:
  0.0 911.9 jit_solution(3556157632553061985)
XLA Ops:
  7.2 26.9 %fusion.22 = (f32[4,64,16,16]{3,2,1,0:T(8,128)}, f32[4,64,16,16]{3,2,1,0:T(8,128)}, f32[4,64,16,16]{3,2,1,0:T(8,128)}, f32[4,64,16,16]{3,2,1,0:T(8,128)}, f32[4,...) fusion(f32[4,64,16,256]{3,2,1,0:T(8,128)} %param.5), kind=kLoop, calls=%fused_computation.53 | loop fusion | bytes 8388608 | tf_op jit(solution)/shard_map/split | solution.py:18
  87.8 14.4 %bitcast_dynamic-update-slice_fusion.12 = f32[16,4,64,16,16]{2,4,3,1,0:T(8,128)} fusion(f32[16,4,64,16,16]{2,4,3,1,0:T(8,128)} %bitcast_dynamic-update-slice_fusion.13, f32[4,64,16,16]{1,3,2,0:T(8,128)} %copy.53), kind=kLoop, calls=%fused_computation.23 | loop fusion | bytes 1048576
  112.3 13.3 %reshape.23 = f32[16,1,65536]{2,1,0:T(1,128)} reshape(f32[16,4,16,16,64]{4,3,2,1,0:T(8,128)} %bitcast.96) | data formatting | bytes 8388608
  125.6 53.2 %all_to_all.23 = f32[16,1,65536]{2,1,0:T(1,128)} all-to-all(f32[16,1,65536]{2,1,0:T(1,128)} %reshape.23), channel_id=1, replica_groups=mesh['gx'=16,'gy'=16] {'gx'}, dimensions={0} | all-to-all | bytes 8388608 | tf_op jit(solution)/shard_map/all_to_all | solution.py:17
  179.4 13.7 %reduce.4 = f32[16,65536]{1,0:T(8,128)} reduce(f32[16,1,65536]{2,1,0:T(1,128)} %all_to_all.23, f32[]{:T(128)} %broadcast.39), dimensions={1}, to_apply=%all_to_all.16.reduce_sub_computation | reduce | bytes 8388612 | tf_op jit(solution)/shard_map/all_to_all | solution.py:17
  193.1 6.9 reshape.24
  203.9 8.1 copy.36
  212.0 7.6 reshape_reshape.3
  219.6 17.6 %bitcast_multiply_fusion = f32[1024,1024]{1,0:T(8,128)} fusion(f32[4,1024,256]{1,2,0:T(8,128)} %reshape_reshape.3), kind=kOutput, calls=%fused_computation | convolution fusion | flops 12885950464 | bytes 8388608 | tf_op jit(solution)/shard_map/sxc,swc->xw/dot_general | solution.py:27
  237.3 273.0 %all-reduce.3.cloned.1.call-done = f32[1024,1024]{1,0:T(8,128)} async-done(((f32[1024,1024]{1,0:T(8,128)}), f32[1024,1024]{1,0:T(8,128)}) %all-reduce.3.cloned.1.call-update) | async-done | bytes 4194320 | tf_op jit(solution)/shard_map/psum | solution.py:26
  510.3 5.6 fusion.23
  517.0 11.7 %cholesky.59 = f32[128,128]{1,0:T(8,128)S(1)} custom-call(f32[128,128]{1,0:T(8,128)S(1)} %fusion.17), custom_call_target="Cholesky" | custom-call | tf_op jit(solution)/shard_map/jit(cholesky)/cholesky | solution.py:32
  530.0 9.8 %custom-call.7 = f32[1,128,128]{1,2,0:T(8,128)S(1)} custom-call(f32[1,128,128]{2,1,0:T(8,128)S(1)} %fusion.9), custom_call_target="InvertDiagBlocksLowerTriangular" | custom-call | tf_op jit(solution)/shard_map/jit(_solve_triangular)/triangular_solve | solution.py:33
  540.5 5.4 fusion.25
  547.0 11.7 %cholesky.70 = f32[128,128]{1,0:T(8,128)S(1)} custom-call(f32[128,128]{1,0:T(8,128)S(1)} %fusion.15), custom_call_target="Cholesky" | custom-call | tf_op jit(solution)/shard_map/jit(cholesky)/cholesky | solution.py:32
  560.1 9.8 %custom-call.8 = f32[1,128,128]{1,2,0:T(8,128)S(1)} custom-call(f32[1,128,128]{2,1,0:T(8,128)S(1)} %fusion.10), custom_call_target="InvertDiagBlocksLowerTriangular" | custom-call | tf_op jit(solution)/shard_map/jit(_solve_triangular)/triangular_solve | solution.py:33
  570.6 5.4 fusion.27
  577.1 11.7 %cholesky.81 = f32[128,128]{1,0:T(8,128)S(1)} custom-call(f32[128,128]{1,0:T(8,128)S(1)} %fusion.13), custom_call_target="Cholesky" | custom-call | tf_op jit(solution)/shard_map/jit(cholesky)/cholesky | solution.py:32
  590.2 9.8 %custom-call.9 = f32[1,128,128]{1,2,0:T(8,128)S(1)} custom-call(f32[1,128,128]{2,1,0:T(8,128)S(1)} %fusion.11), custom_call_target="InvertDiagBlocksLowerTriangular" | custom-call | tf_op jit(solution)/shard_map/jit(_solve_triangular)/triangular_solve | solution.py:33
  600.6 5.2 fusion.1
  605.9 4.4 copy.42
  613.8 21.2 %all_to_all.24 = f32[16,1,8192]{2,1,0:T(1,128)S(1)} all-to-all(f32[16,1,8192]{2,1,0:T(1,128)S(1)} %reshape.25), channel_id=1, replica_groups=mesh['gx'=16,'gy'=16] {'gy'}, dimensions={0} | all-to-all | bytes 1048576 | tf_op jit(solution)/shard_map/all_to_all | solution.py:36
  639.6 5.6 copy.44
  651.5 251.6 %all-reduce.5.cloned.1.call-done = f32[256,256]{1,0:T(8,128)} async-done(((f32[256,256]{1,0:T(8,128)}), f32[256,256]{1,0:T(8,128)}) %all-reduce.5.cloned.1.call-update) | async-done | bytes 262160 | tf_op jit(solution)/shard_map/psum | solution.py:38
  (90 shorter events, 93.6 us)
Async XLA Ops:
  7.2 503.1 %copy-start = (f32[1024,128]{1,0:T(8,128)S(1)}, f32[1024,128]{1,0:T(8,128)}, u32[]{:S(2)}) copy-start(f32[1024,128]{1,0:T(8,128)} %param.6) | copy-start | bytes 1572868
  7.2 503.1 %all-reduce.3.cloned.1.call-start = ((), (), s32[]{:S(2)}) async-start(), calls=%async_computation.2 | async-start | bytes 8388608 | tf_op jit(solution)/shard_map/psum | solution.py:26
  81.9 20.3 %copy-start.11 = (f32[4,64,16,16]{1,3,2,0:T(8,128)S(1)}, f32[4,64,16,16]{1,3,2,0:T(8,128)}, u32[]{:S(2)}) copy-start(f32[4,64,16,16]{1,3,2,0:T(8,128)} %copy.54) | copy-start | bytes 786436
  81.9 21.1 %copy-start.10 = (f32[4,64,16,16]{1,3,2,0:T(8,128)S(1)}, f32[4,64,16,16]{1,3,2,0:T(8,128)}, u32[]{:S(2)}) copy-start(f32[4,64,16,16]{1,3,2,0:T(8,128)} %copy.55) | copy-start | bytes 786436
  81.9 22.0 %copy-start.9 = (f32[4,64,16,16]{1,3,2,0:T(8,128)S(1)}, f32[4,64,16,16]{1,3,2,0:T(8,128)}, u32[]{:S(2)}) copy-start(f32[4,64,16,16]{1,3,2,0:T(8,128)} %copy.56) | copy-start | bytes 786436
  81.9 22.8 %copy-start.8 = (f32[4,64,16,16]{1,3,2,0:T(8,128)S(1)}, f32[4,64,16,16]{1,3,2,0:T(8,128)}, u32[]{:S(2)}) copy-start(f32[4,64,16,16]{1,3,2,0:T(8,128)} %copy.57) | copy-start | bytes 786436
  81.9 23.7 %copy-start.7 = (f32[4,64,16,16]{1,3,2,0:T(8,128)S(1)}, f32[4,64,16,16]{1,3,2,0:T(8,128)}, u32[]{:S(2)}) copy-start(f32[4,64,16,16]{1,3,2,0:T(8,128)} %copy.58) | copy-start | bytes 786436
  83.9 22.5 %copy-start.6 = (f32[4,64,16,16]{1,3,2,0:T(8,128)S(1)}, f32[4,64,16,16]{1,3,2,0:T(8,128)}, u32[]{:S(2)}) copy-start(f32[4,64,16,16]{1,3,2,0:T(8,128)} %copy.59) | copy-start | bytes 786436
  85.8 21.4 %copy-start.5 = (f32[4,64,16,16]{1,3,2,0:T(8,128)S(1)}, f32[4,64,16,16]{1,3,2,0:T(8,128)}, u32[]{:S(2)}) copy-start(f32[4,64,16,16]{1,3,2,0:T(8,128)} %copy.60) | copy-start | bytes 786436
  87.8 20.3 %copy-start.4 = (f32[4,64,16,16]{1,3,2,0:T(8,128)S(1)}, f32[4,64,16,16]{1,3,2,0:T(8,128)}, u32[]{:S(2)}) copy-start(f32[4,64,16,16]{1,3,2,0:T(8,128)} %copy.61) | copy-start | bytes 786436
  102.2 6.8 copy-start.3
  103.0 6.8 copy-start.2
  103.9 6.8 copy-start.1
  237.2 665.9 %all-reduce.5.cloned.1.call-start = ((), (), s32[]{:S(2)}) async-start(), calls=%async_computation.3 | async-start | bytes 524288 | tf_op jit(solution)/shard_map/psum | solution.py:38
Sparse Core Ops, SparseCore 0:
  237.3 272.8 all-reduce.2
  650.6 252.4 all-reduce.4

commit v2 on v0

--- a/solution.py
+++ b/solution.py
@@ -30,7 +30,7 @@
     core_blocks = core_tensor.reshape(species, R, cols_y, slab_z)
     blocks = lax.all_to_all(core_blocks, "gy", split_axis=1, concat_axis=2, tiled=True)
     second_part = jnp.einsum("sryz,srwz->yw", blocks, blocks, precision=highest) / (S * R * NZ)
-    gram_two = lax.psum(second_part, ("gx", "gy"))
+    gram_two = jnp.sum(lax.all_gather(second_part, ("gx", "gy")), axis=0)
     return (basis * math.sqrt(rows_x), gram_two)
 
 

time: 826 us -> 1390 us (1.68)
  waiting for transfers between devices: 525 us -> 1060 us
  other arithmetic: 84.2 us -> 106 us
    all_gather x0 -> x1, waiting for transfers between devices: none -> 786 us  [body(): gram_two = jnp.sum(lax.all_gather(second_part, ('gx', 'gy')), axis=0)]
    psum x1 -> x0, waiting for transfers between devices: 252 us -> none  [body(): gram_two = lax.psum(second_part, ('gx', 'gy'))]
    reduce_sum x0 -> x1, other arithmetic: none -> 21.8 us  [body(): gram_two = jnp.sum(lax.all_gather(second_part, ('gx', 'gy')), axis=0)]
    unnamed x9 -> x10, local copies, waits for them, and re-layouts: 38.3 us -> 36.6 us
where the time goes in v2:
time: 1390 us; the launch traced here: 1370 us
  waiting for transfers between devices  1060 us (76%)
  other arithmetic  106 us (8%)
  blocking collectives  74.2 us (5%)
  local copies, waits for them, and re-layouts  70.4 us (5%)
  matrix products  47.4 us (3%)
  between operations  14.7 us (1%)
    all_gather x1, waiting for transfers between devices, body(): gram_two = jnp.sum(lax.all_gather(second_part, ('gx', 'gy')), axis=0)  786 us
    psum x1, waiting for transfers between devices, body(): lax.psum(jnp.einsum('sxc,swc->xw', fibers, fibers, precision=highest) * s...  273 us
    all_to_all x1, blocking collectives, body(): lax.all_to_all(species_field, 'gx', split_axis=3, concat_axis=1, tiled=True)  53.2 us
    another operation x9, other arithmetic, body(): factor_low = jnp.linalg.cholesky(square)  37.2 us
    unnamed x10, local copies, waits for them, and re-layouts  36.6 us
    another operation x6, other arithmetic, body(): basis = jax.scipy.linalg.solve_triangular(factor_low, wide.T, lower=True).T  31.4 us
  transfers between devices with their start and end apart: 2, of which 2 were waited for; matrix products, arithmetic and copies ran while one was open for 0% of the time, Pallas kernels for 0%

profile of v2, /device:TPU:2, one launch (start us, length us, event | category | flops | bytes accessed | tf_op | source)
XLA Modules:
  0.0 1372.0 jit_solution(1374984329752968847)
XLA Ops:
  7.2 9.2 copy.33
  16.4 13.3 reshape.25
  29.7 53.2 %all_to_all.33 = f32[16,1,65536]{2,1,0:T(1,128)} all-to-all(f32[16,1,65536]{2,1,0:T(1,128)} %reshape.25), channel_id=1, replica_groups=mesh['gx'=16,'gy'=16] {'gx'}, dimensions={0} | all-to-all | bytes 8388608 | tf_op jit(solution)/shard_map/all_to_all | solution.py:16
  83.4 13.7 reduce.4
  97.2 6.9 reshape.26
  104.1 11.4 copy.35
  115.5 7.6 reshape.19
  123.1 17.8 %bitcast_multiply_fusion = f32[1024,1024]{1,0:T(8,128)} fusion(f32[4,1024,256]{1,2,0:T(8,128)} %reshape.19), kind=kOutput, calls=%fused_computation | convolution fusion | flops 12885950464 | bytes 8388608 | tf_op jit(solution)/shard_map/sxc,swc->xw/dot_general | solution.py:22
  141.0 273.0 %all-reduce.2.cloned.1.call-done = f32[1024,1024]{1,0:T(8,128)} async-done(((f32[1024,1024]{1,0:T(8,128)}), f32[1024,1024]{1,0:T(8,128)}) %all-reduce.2.cloned.1.call-update) | async-done | bytes 4194320 | tf_op jit(solution)/shard_map/psum | solution.py:21
  414.0 5.6 fusion.21
  420.7 11.7 cholesky.59
  433.8 9.8 custom-call.7
  444.3 5.4 fusion.23
  450.8 11.7 cholesky.70
  463.8 9.8 custom-call.8
  474.3 5.4 fusion.25
  480.9 11.7 cholesky.81
  493.9 9.8 custom-call.9
  504.4 6.5 convolution_bitcast_fusion
  511.1 4.6 copy.43
  519.3 21.0 %all_to_all.34 = f32[16,1,8192]{2,1,0:T(1,128)S(1)} all-to-all(f32[16,1,8192]{2,1,0:T(1,128)S(1)} %reshape.27), channel_id=1, replica_groups=mesh['gx'=16,'gy'=16] {'gy'}, dimensions={0} | all-to-all | bytes 1048576 | tf_op jit(solution)/shard_map/all_to_all | solution.py:31
  544.9 5.6 copy.45
  556.7 786.2 %all-gather.3.cloned.1.call-done = f32[65536,256]{1,0:T(8,128)} async-done(((f32[256,256]{1,0:T(8,128)}), f32[65536,256]{1,0:T(8,128)}) %all-gather.3.cloned.1.call-update) | async-done | bytes 67108880 | tf_op jit(solution)/shard_map/all_gather | solution.py:33
  1342.9 21.8 %reduce_sum.9 = f32[256,256]{1,0:T(8,128)} reduce(f32[256,256,256]{2,1,0:T(8,128)} %bitcast.25, f32[]{:T(128)} %constant.39.clone.1), dimensions={0}, to_apply=%region_3.6 | reduce | flops 16711680 | bytes 67371008 | tf_op jit(solution)/shard_map/reduce_sum | solution.py:33
  (38 shorter events, 24.5 us)
Async XLA Ops:
  7.2 406.8 %copy-start = (f32[1024,128]{1,0:T(8,128)S(1)}, f32[1024,128]{1,0:T(8,128)}, u32[]{:S(2)}) copy-start(f32[1024,128]{1,0:T(8,128)} %param.6) | copy-start | bytes 1572868
  7.2 406.8 %all-reduce.2.cloned.1.call-start = ((), (), s32[]{:S(2)}) async-start(), calls=%async_computation.2 | async-start | bytes 8388608 | tf_op jit(solution)/shard_map/psum | solution.py:21
  140.9 1202.0 %all-gather.3.cloned.1.call-start = ((), (), s32[]{:S(2)}) async-start(), calls=%async_computation.3 | async-start | bytes 67371008 | tf_op jit(solution)/shard_map/all_gather | solution.py:33
  1342.9 21.8 %copy-start.1 = (f32[1024,128]{1,0:T(8,128)S(1)}, f32[1024,128]{1,0:T(8,128)}, u32[]{:S(2)}) copy-start(f32[1024,128]{1,0:T(8,128)} %param.6) | copy-start | bytes 1572868
Sparse Core Ops, SparseCore 0:
  141.0 272.9 all-reduce.1
  555.8 787.0 all-gather.2
